TPU v7x, 128 devices: a whole 4x4x4 slice. The times are simulated.
128 devices in a mesh: dp: 32 (over y, x, core), tensor: 4 (over z).
Axes of the slice: x: 4, y: 4, z: 4, core: 2. Of those that a mesh axis runs over, the one named last changes fastest.
Arguments:
- layer_input: bfloat16 [4096, 2560], P('dp'), may hold values from -6 to 6
- inner_out: bfloat16 [4096, 2560], P('dp', 'tensor'), may hold values from -6 to 6
- out_grad: bfloat16 [4096, 2560], P('dp'), may hold values from -0.09375 to 0.09375
- zx_grad: bfloat16 [4096, 5120], P('dp', 'tensor'), may hold values from -0.09375 to 0.09375
- bc_grad: bfloat16 [4096, 1024], P('dp', 'tensor'), may hold values from -0.09375 to 0.09375
- dt_grad: bfloat16 [4096, 40], P('dp', 'tensor'), may hold values from -0.09375 to 0.09375
- owner_deal: int32 [4, 31], P('tensor'), may hold values from 0 to 31, as said below
- head_momentum: float32 [4, 2368, 2560], P('tensor', 'dp'), may hold values from -6 to 6
- bc_momentum: float32 [2, 128, 2560], replicated, may hold values from -6 to 6
Outputs:
- head_update: bfloat16 [40, 3, 64, 2560], P('tensor')
- dt_update: bfloat16 [40, 2560], P('tensor')
- bc_update: bfloat16 [2, 128, 2560], replicated
- head_momentum_out: float32 [4, 2368, 2560], P('tensor', 'dp')
- bc_momentum_out: float32 [2, 128, 2560], replicated
Inputs may be any that keep to these rules, and one draw needn't show every extreme that they name: `owner_deal`: each owner holds at most 1 head blocks of one tensor index; the owner of the dt block (the last entry) holds exactly 1 head blocks of that index as well, so it holds exactly 74 rows.
All inputs are finite; a program needn't handle non-finite values.
Results may differ from a plain program's by a relative error of at most 0.0085.
Values may be sent and summed in bfloat16 or wider, within the bound.
No kernel may reach another device: no remote copies, remote signals or barrier semaphores. Data moves between devices by JAX's collectives and lax.ppermute only.
A program may use at most 128 MiB of HBM per device.

v0:
```python
import math
import jax
import jax.numpy as jnp
from jax import lax
from jax.sharding import PartitionSpec as P

HD = 64
STATE = 128
NS_ITERS = 5
quintic_first = 3.4445
quintic_second = -4.775
quintic_third = 2.0315
momentum_decay = 0.95
norm_epsilon = 1e-07
HEAD_REDUCE = "all_to_all"


def orthogonalize(moment):
    highest = lax.Precision.HIGHEST
    norm_value = jnp.sqrt(jnp.sum(moment * moment, axis=(1, 2), keepdims=True))
    current = moment / (norm_value + norm_epsilon)
    for step in range(NS_ITERS):
        gram_matrix = jnp.einsum("bik,bjk->bij", current, current, precision=highest)
        polynomial = quintic_second * gram_matrix + quintic_third * jnp.einsum(
            "bij,bjk->bik", gram_matrix, gram_matrix, precision=highest
        )
        current = quintic_first * current + jnp.einsum(
            "bij,bjk->bik", polynomial, current, precision=highest
        )
    return current


def on_device(
    layer_input,
    inner_out,
    out_grad,
    zx_grad,
    bc_grad,
    dt_grad,
    owner_deal,
    head_momentum,
    bc_momentum,
):
    n_data = lax.axis_size("dp")
    tokens, width = layer_input.shape
    heads_here = dt_grad.shape[1]
    capacity = head_momentum.shape[1]
    n_blocks = 3 * heads_here
    contract = (((0,), (0,)), ((), ()))
    f32, bf16 = (jnp.float32, jnp.bfloat16)
    owners = owner_deal[0]
    head_owner = owners[:n_blocks]
    dt_owner = owners[n_blocks]
    slots = jnp.arange(n_data, dtype=jnp.int32)
    bc_cols = lax.psum(bc_grad.astype(f32), "tensor")
    bc_part = lax.dot_general(
        bc_cols,
        layer_input.astype(f32),
        contract,
        precision=lax.Precision.HIGHEST,
        preferred_element_type=f32,
    )
    bc_summed = lax.psum(bc_part, "dp")
    zx = zx_grad.reshape(tokens, heads_here, 2, HD)
    io = inner_out.reshape(tokens, heads_here, 1, HD)
    upper = jnp.concatenate([zx, jnp.zeros_like(io)], axis=2).reshape(tokens, n_blocks, HD)
    lower = jnp.concatenate([jnp.zeros_like(zx), io], axis=2).reshape(tokens, n_blocks, HD)
    grad_blocks = jnp.concatenate([upper, lower], axis=0)
    pick = (head_owner[None, :] == slots[:, None]).astype(bf16)
    owner_cols = jnp.einsum("tbr,ob->tor", grad_blocks, pick, preferred_element_type=f32).astype(
        bf16
    )
    dt_cols = jnp.concatenate([dt_grad, jnp.zeros_like(dt_grad)], axis=0)
    is_dt = (slots == dt_owner).astype(bf16)
    dt_owner_cols = dt_cols[:, None, :] * is_dt[None, :, None]
    send_cols = jnp.concatenate([owner_cols, dt_owner_cols], axis=2).reshape(
        2 * tokens, n_data * capacity
    )
    factors = jnp.concatenate([layer_input, out_grad], axis=0)
    send = lax.dot_general(send_cols, factors, contract, preferred_element_type=f32).astype(bf16)
    if HEAD_REDUCE == "all_to_all":
        received = lax.all_to_all(send, "dp", split_axis=0, concat_axis=0, tiled=True)
        owned_sum = jnp.sum(received.reshape(n_data, capacity, width).astype(f32), axis=0)
    else:
        owned_sum = lax.psum_scatter(send, "dp", scatter_dimension=0, tiled=True).astype(f32)
    moment = momentum_decay * head_momentum[0] + owned_sum
    head_direction = orthogonalize(moment[None, :HD])[0]
    dt_direction = orthogonalize(moment[None, HD:])[0]
    owned_update = (
        jnp.concatenate([head_direction, dt_direction], axis=0) * math.sqrt(width)
    ).astype(bf16)
    everything = lax.all_gather(owned_update, "dp", axis=0, tiled=False)
    head_update = jnp.take(everything[:, :HD], head_owner, axis=0, mode="clip").reshape(
        heads_here, 3, HD, width
    )
    dt_update = lax.dynamic_index_in_dim(everything, dt_owner, axis=0, keepdims=False)[HD:]
    bc_moment = momentum_decay * bc_momentum + bc_summed.reshape(2, STATE, width)
    bc_update = (orthogonalize(bc_moment) * math.sqrt(width)).astype(bf16)
    return (head_update, dt_update, bc_update, moment[None], bc_moment)


def solution(mesh):
    in_specs = (
        P("dp", None),
        P("dp", "tensor"),
        P("dp", None),
        P("dp", "tensor"),
        P("dp", "tensor"),
        P("dp", "tensor"),
        P("tensor", None),
        P("tensor", "dp", None),
        P(),
    )
    out_specs = (
        P("tensor", None, None, None),
        P("tensor", None),
        P(),
        P("tensor", "dp", None),
        P(),
    )
    return jax.shard_map(
        on_device, mesh=mesh, in_specs=in_specs, out_specs=out_specs, check_vma=False
    )
```

profile of v0, /device:TPU:1, one launch (start us, length us, event | category | flops | bytes accessed | tf_op | source)
XLA Modules:
  0.0 375.3 jit_solution(5837344694989984997)
XLA Ops:
  7.2 1.2 slice.24
  8.4 0.7 slice_bitcast_fusion
  9.1 0.6 compare_convert_fusion
  9.7 1.1 copy.28
  10.8 0.7 concatenate.35
  11.9 1.2 copy.27
  13.2 0.3 copy.30
  13.6 0.4 fusion.4
  14.1 0.7 copy.32
  14.8 0.4 reshape.316
  15.2 7.2 %convolution_convert_fusion = bf16[2368,2560]{1,0:T(8,128)(2,1)} fusion(bf16[256,2368]{0,1:T(8,128)(2,1)S(1)} %reshape.316, bf16[128,2560]{1,0:T(8,128)(2,1)} %param.11, bf16[128,2560]{1,0:T(8,128)(2,1)S(1)} %copy-done.1), kind=kOutput, calls=%fused_computation.2 | convolution fusion | flops 3112468480 | bytes 14647296 | tf_op jit(solution)/shard_map/dot_general | solution.py:80
  22.4 12.3 %all_to_all.6 = bf16[32,74,2560]{2,1,0:T(8,128)(2,1)} reshape(bf16[2368,2560]{1,0:T(8,128)(2,1)} %convolution_convert_fusion) | data formatting | bytes 24248320 | tf_op jit(solution)/shard_map/all_to_all | solution.py:82
  34.7 8.8 %all-to-all-start = ((bf16[32,74,2560]{2,1,0:T(8,128)(2,1)}), bf16[32,74,2560]{2,1,0:T(8,128)(2,1)}, u32[]{:S(2)}, u32[]{:S(2)}) async-start(bf16[32,74,2560]{2,1,0:T(8,128)(2,1)} %all_to_all.6), calls=%async_computation | async-start | bytes 26214400 | tf_op jit(solution)/shard_map/all_to_all | solution.py:82
  43.5 17.5 %all-reduce.7 = f32[128,256]{1,0:T(8,128)S(1)} all-reduce(bf16[128,256]{1,0:T(8,128)(2,1)S(1)} %copy-done.3), channel_id=1, replica_groups=mesh['dp'=32,'tensor'=4] {'tensor'}, use_global_device_ids=true, to_apply=%region_3.0 | all-reduce | flops 32768 | bytes 196608 | tf_op jit(solution)/shard_map/psum | solution.py:55
  61.0 2.7 fusion.43
  63.8 0.6 all-gather.2.cloned.1.call-start
  64.3 139.2 %all-to-all-done = bf16[32,74,2560]{2,1,0:T(8,128)(2,1)} async-done(((bf16[32,74,2560]{2,1,0:T(8,128)(2,1)}), bf16[32,74,2560]{2,1,0:T(8,128)(2,1)}, u32[]{:S(2)}, u32[]{:S(2)}) %all-to-all-start) | async-done | bytes 12124192 | tf_op jit(solution)/shard_map/all_to_all | solution.py:82
  203.6 6.8 %convert_reduce_fusion = f32[74,2560]{1,0:T(8,128)S(1)} fusion(bf16[32,74,2560]{2,1,0:T(8,128)(2,1)} %all-to-all-done), kind=kLoop, calls=%fused_computation.1 | loop fusion | flops 11934720 | bytes 12881920 | tf_op jit(solution)/shard_map/reduce_sum | solution.py:83
  210.6 0.6 multiply_reduce_fusion.2
  211.2 0.8 multiply_reduce_fusion.1
  213.8 0.7 fusion.28
  215.0 0.7 convolution_add_fusion.9
  218.5 0.7 fusion.35
  219.3 0.7 convolution_add_fusion.8
  220.0 0.7 fusion.36
  220.9 0.7 convolution_add_fusion.7
  221.6 0.7 fusion.37
  222.7 0.7 convolution_add_fusion.6
  223.4 0.7 fusion.38
  224.2 0.7 fusion.2
  224.9 0.8 fusion.26
  227.7 53.1 %all-reduce.6.cloned.1.call-done = f32[2,128,2560]{2,1,0:T(8,128)} async-done(((f32[2,128,2560]{2,1,0:T(8,128)}), f32[2,128,2560]{2,1,0:T(8,128)}) %all-reduce.6.cloned.1.call-update) | async-done | bytes 2621456 | tf_op jit(solution)/shard_map/psum | solution.py:63
  280.9 3.2 multiply_reduce_fusion
  284.0 2.9 fusion.27
  287.3 2.7 convolution_add_fusion.4
  289.9 2.5 fusion.44
  292.7 2.6 convolution_add_fusion.3
  295.4 2.7 fusion.45
  298.4 2.6 convolution_add_fusion.2
  301.0 2.5 fusion.46
  303.8 2.6 convolution_add_fusion.1
  306.5 2.5 fusion.47
  309.3 4.0 %fusion.1 = bf16[2,128,2560]{2,1,0:T(8,128)(2,1)} fusion(f32[2,128,128]{2,1,0:T(8,128)S(1)} %fusion.8, f32[2,128,2560]{2,1,0:T(8,128)S(1)} %convolution_add_fusion.1), kind=kOutput, calls=%fused_computation.9 | convolution fusion | flops 1009254400 | bytes 4063232 | tf_op jit(solution)/shard_map/bij,bjk->bik/dot_general | solution.py:27
  313.4 1.6 copy.33
  315.0 32.9 %all-gather.2.cloned.1.call-done = bf16[32,74,2560]{2,1,0:T(8,128)(2,1)} async-done(((bf16[1,74,2560]{2,1,0:T(8,128)(2,1)}), bf16[32,74,2560]{2,1,0:T(8,128)(2,1)}) %all-gather.2.cloned.1.call-update) | async-done | bytes 12124176 | tf_op jit(solution)/shard_map/all_gather | solution.py:92
  347.9 9.0 %slice.34 = bf16[32,64,2560]{2,1,0:T(8,128)(2,1)} slice(bf16[32,74,2560]{2,1,0:T(8,128)(2,1)} %all-gather.2.cloned.1.call-done), slice={[0:32], [0:64], [0:2560]} | slice | bytes 20971520 | tf_op jit(solution)/shard_map/slice | solution.py:93
  356.8 9.9 %gather_fusion = bf16[30,64,2560]{2,1,0:T(8,128)(2,1)} fusion(bf16[32,64,2560]{2,1,0:T(8,128)(2,1)} %slice.34, s32[1024]{0:T(1024)S(1)} %pad_clamp_fusion), kind=kCustom, calls=%fused_computation | custom fusion | bytes 19660920 | tf_op jit(solution)/shard_map/jit(_take)/gather | solution.py:93
  366.7 1.5 dynamic-slice_bitcast_fusion
  (45 shorter events, 7.0 us)
Async XLA Ops:
  14.1 1.1 copy-start.1
  34.7 8.8 %copy-start.3 = (bf16[128,256]{1,0:T(8,128)(2,1)S(1)}, bf16[128,256]{1,0:T(8,128)(2,1)}, u32[]{:S(2)}) copy-start(bf16[128,256]{1,0:T(8,128)(2,1)} %param.13) | copy-start | bytes 196612
  34.7 168.9 %all-to-all-start = ((bf16[32,74,2560]{2,1,0:T(8,128)(2,1)}), bf16[32,74,2560]{2,1,0:T(8,128)(2,1)}, u32[]{:S(2)}, u32[]{:S(2)}) async-start(bf16[32,74,2560]{2,1,0:T(8,128)(2,1)} %all_to_all.6), calls=%async_computation | async-start | bytes 26214400 | tf_op jit(solution)/shard_map/all_to_all | solution.py:82
  43.5 237.4 %all-reduce.6.cloned.1.call-start = ((), (), s32[]{:S(2)}) async-start(), calls=%async_computation.2 | async-start | bytes 5242880 | tf_op jit(solution)/shard_map/psum | solution.py:63
  63.8 146.7 %copy-start = (f32[1,74,2560]{2,0,1:T(1,128)S(1)}, f32[1,74,2560]{2,0,1:T(1,128)}, u32[]{:S(2)}) copy-start(f32[1,74,2560]{2,0,1:T(1,128)} %param.16) | copy-start | bytes 2273284
  63.8 284.1 %all-gather.2.cloned.1.call-start = ((), (), s32[]{:S(2)}) async-start(), calls=%async_computation.1 | async-start | bytes 13516800 | tf_op jit(solution)/shard_map/all_gather | solution.py:92
  284.0 3.2 copy-start.2
Sparse Core Ops, SparseCore 0:
  63.9 216.9 all-reduce.5
  283.7 64.1 all-gather.1
where the time goes:
time: 381 us; the launch traced here: 375 us
  waiting for transfers between devices  225 us (59%)
  matrix products  50.9 us (13%)
  local copies, waits for them, and re-layouts  41 us (11%)
  between operations  18 us (5%)
  blocking collectives  17.5 us (5%)
  other arithmetic  13.3 us (3%)
  starting transfers between devices  9.36 us (2%)
    all_to_all x1, waiting for transfers between devices, on_device(): lax.all_to_all(send, 'dp', split_axis=0, concat_axis=0, tiled=True)  139 us
    psum x1, waiting for transfers between devices, on_device(): bc_summed = lax.psum(bc_part, 'dp')  53.1 us
    all_gather x1, waiting for transfers between devices, on_device(): everything = lax.all_gather(owned_update, 'dp', axis=0, tiled=False)  32.9 us
    dot_general x15, matrix products, orthogonalize(): jnp.einsum('bij,bjk->bik', polynomial, current, precision=highest)  19.5 us
    dot_general x15, matrix products, orthogonalize(): jnp.einsum('bik,bjk->bij', current, current, precision=highest)  18 us
    psum x1, blocking collectives, on_device(): bc_cols = lax.psum(bc_grad.astype(f32), 'tensor')  17.5 us
    all_to_all x1, local copies, waits for them, and re-layouts, on_device(): lax.all_to_all(send, 'dp', split_axis=0, concat_axis=0, tiled=True)  12.3 us
    gather x1, local copies, waits for them, and re-layouts, on_device(): jnp.take(everything[:, :HD], head_owner, axis=0, mode='clip')  9.86 us
  transfers between devices with their start and end apart: 3, of which 3 were waited for; matrix products, arithmetic and copies ran while one was open for 15% of the time, Pallas kernels for 0%

commit v1 on v0

--- a/solution.py
+++ b/solution.py
@@ -41,6 +41,15 @@
     head_momentum,
     bc_momentum,
 ):
+
+    def fill_plate(vec):
+        ndev = lax.axis_size("dp")
+        all_values = vec
+        for dd in [[(k, k ^ t) for k in range(ndev)] for t in (1, 2, 4, 8, 16) if t < ndev]:
+            v1 = lax.ppermute(all_values, perm=dd, axis_name="dp")
+            all_values = all_values + v1
+        return all_values
+
     n_data = lax.axis_size("dp")
     tokens, width = layer_input.shape
     heads_here = dt_grad.shape[1]
@@ -60,7 +69,7 @@
         precision=lax.Precision.HIGHEST,
         preferred_element_type=f32,
     )
-    bc_summed = lax.psum(bc_part, "dp")
+    bc_summed = fill_plate(bc_part)
     zx = zx_grad.reshape(tokens, heads_here, 2, HD)
     io = inner_out.reshape(tokens, heads_here, 1, HD)
     upper = jnp.concatenate([zx, jnp.zeros_like(io)], axis=2).reshape(tokens, n_blocks, HD)

time: 381 us -> 564 us (1.48)
  blocking collectives: 17.5 us -> 172 us
  waiting for transfers between devices: 225 us -> 254 us
    ppermute x0 -> x5, waiting for transfers between devices: none -> 254 us  [fill_plate(): v1 = lax.ppermute(all_values, perm=dd, axis_name='dp')]
    all_to_all x0 -> x1, blocking collectives: none -> 155 us  [on_device(): lax.all_to_all(send, 'dp', split_axis=0, concat_axis=0, tiled=True)]
    all_to_all x1 -> x0, waiting for transfers between devices: 139 us -> none  [on_device(): lax.all_to_all(send, 'dp', split_axis=0, concat_axis=0, tiled=True)]
    psum x1 -> x0, waiting for transfers between devices: 53.1 us -> none  [on_device(): bc_summed = lax.psum(bc_part, 'dp')]
    all_gather x1, waiting for transfers between devices: 32.9 us -> 0.01 us  [on_device(): everything = lax.all_gather(owned_update, 'dp', axis=0, tiled=False)]
    all_to_all x1 -> x0, starting transfers between devices: 8.75 us -> none  [on_device(): lax.all_to_all(send, 'dp', split_axis=0, concat_axis=0, tiled=True)]
    ppermute x0 -> x5, starting transfers between devices: none -> 6.75 us  [fill_plate(): v1 = lax.ppermute(all_values, perm=dd, axis_name='dp')]
  transfers between devices with their start and end apart: 3 -> 6, of which waited for: 3 -> 5; matrix products, arithmetic and copies ran while one was open for 15% -> 7% of each run, Pallas kernels for 0% -> 0%
where the time goes in v1:
time: 564 us; the launch traced here: 557 us
  waiting for transfers between devices  254 us (45%)
  blocking collectives  172 us (30%)
  matrix products  49.9 us (9%)
  local copies, waits for them, and re-layouts  41.1 us (7%)
  between operations  18.3 us (3%)
  other arithmetic  15.3 us (3%)
  starting transfers between devices  6.79 us (1%)
    ppermute x5, waiting for transfers between devices, fill_plate(): v1 = lax.ppermute(all_values, perm=dd, axis_name='dp')  254 us
    all_to_all x1, blocking collectives, on_device(): lax.all_to_all(send, 'dp', split_axis=0, concat_axis=0, tiled=True)  155 us
    dot_general x15, matrix products, orthogonalize(): jnp.einsum('bij,bjk->bik', polynomial, current, precision=highest)  19.5 us
    dot_general x15, matrix products, orthogonalize(): jnp.einsum('bik,bjk->bij', current, current, precision=highest)  18.4 us
    psum x1, blocking collectives, on_device(): bc_cols = lax.psum(bc_grad.astype(f32), 'tensor')  16.1 us
    all_to_all x1, local copies, waits for them, and re-layouts, on_device(): lax.all_to_all(send, 'dp', split_axis=0, concat_axis=0, tiled=True)  12.3 us
  transfers between devices with their start and end apart: 6, of which 5 were waited for; matrix products, arithmetic and copies ran while one was open for 7% of the time, Pallas kernels for 0%

profile of v1, /device:TPU:1, one launch (start us, length us, event | category | flops | bytes accessed | tf_op | source)
XLA Modules:
  0.0 556.9 jit_solution(14770461843253979926)
XLA Ops:
  7.2 1.2 slice.24
  9.8 1.1 copy.28
  10.8 0.7 concatenate.35
  12.0 1.2 copy.27
  14.2 0.7 copy.32
  15.3 7.2 %convolution_convert_fusion = bf16[2368,2560]{1,0:T(8,128)(2,1)} fusion(bf16[256,2368]{0,1:T(8,128)(2,1)S(1)} %reshape.316, bf16[128,2560]{1,0:T(8,128)(2,1)} %param.11, bf16[128,2560]{1,0:T(8,128)(2,1)S(1)} %copy-done.1), kind=kOutput, calls=%fused_computation.2 | convolution fusion | flops 3112468480 | bytes 14647296 | tf_op jit(solution)/shard_map/dot_general | solution.py:89
  22.4 12.3 %all_to_all.6 = bf16[32,74,2560]{2,1,0:T(8,128)(2,1)} reshape(bf16[2368,2560]{1,0:T(8,128)(2,1)} %convolution_convert_fusion) | data formatting | bytes 24248320 | tf_op jit(solution)/shard_map/all_to_all | solution.py:91
  34.8 155.5 %all_to_all.9 = bf16[32,74,2560]{2,1,0:T(8,128)(2,1)} all-to-all(bf16[32,74,2560]{2,1,0:T(8,128)(2,1)} %all_to_all.6), channel_id=1, replica_groups=mesh['dp'=32,'tensor'=4] {'dp'}, dimensions={0} | all-to-all | bytes 24248320 | tf_op jit(solution)/shard_map/all_to_all | solution.py:91
  190.3 6.9 %convert_reduce_fusion = f32[74,2560]{1,0:T(8,128)S(1)} fusion(bf16[32,74,2560]{2,1,0:T(8,128)(2,1)} %all_to_all.9), kind=kLoop, calls=%fused_computation.1 | loop fusion | flops 11934720 | bytes 12881920 | tf_op jit(solution)/shard_map/reduce_sum | solution.py:92
  197.9 0.8 multiply_reduce_fusion.1
  200.6 0.7 fusion.28
  201.7 0.7 convolution_add_fusion.8
  205.5 0.7 fusion.39
  206.3 0.7 convolution_add_fusion.7
  207.0 0.7 fusion.40
  207.9 0.7 convolution_add_fusion.6
  208.6 0.7 fusion.41
  209.4 0.7 convolution_add_fusion.5
  210.1 0.7 fusion.42
  211.0 0.7 fusion.2
  211.7 0.8 fusion.27
  212.5 16.1 %all-reduce.4 = f32[128,256]{1,0:T(8,128)S(1)} all-reduce(bf16[128,256]{1,0:T(8,128)(2,1)S(1)} %copy-done.5), channel_id=1, replica_groups=mesh['dp'=32,'tensor'=4] {'tensor'}, use_global_device_ids=true, to_apply=%region_3.0 | all-reduce | flops 32768 | bytes 196608 | tf_op jit(solution)/shard_map/psum | solution.py:64
  228.6 1.2 fusion.47
  229.8 4.2 collective-permute-start
  234.1 4.5 collective-permute-done
  239.3 84.1 %collective-permute-done.1 = f32[256,2560]{1,0:T(8,128)S(1)} collective-permute-done((f32[256,2560]{1,0:T(8,128)S(1)}, f32[256,2560]{1,0:T(8,128)S(1)}, u32[]{:S(2)}, u32[]{:S(2)}) %collective-permute-start.1) | collective-permute-done | bytes 2621472 | tf_op jit(solution)/shard_map/ppermute | solution.py:49
  323.7 1.2 collective-permute-start.2
  324.9 57.6 %collective-permute-done.2 = f32[256,2560]{1,0:T(8,128)S(1)} collective-permute-done((f32[256,2560]{1,0:T(8,128)S(1)}, f32[256,2560]{1,0:T(8,128)S(1)}, u32[]{:S(2)}, u32[]{:S(2)}) %collective-permute-start.2) | collective-permute-done | bytes 2621472 | tf_op jit(solution)/shard_map/ppermute | solution.py:49
  382.9 56.3 %collective-permute-done.3 = f32[256,2560]{1,0:T(8,128)S(1)} collective-permute-done((f32[256,2560]{1,0:T(8,128)S(1)}, f32[256,2560]{1,0:T(8,128)S(1)}, u32[]{:S(2)}, u32[]{:S(2)}) %collective-permute-start.3) | collective-permute-done | bytes 2621472 | tf_op jit(solution)/shard_map/ppermute | solution.py:49
  439.5 0.9 collective-permute-start.4
  442.4 1.2 bitcast_add_fusion
  443.7 1.6 copy.33
  445.3 51.4 %collective-permute-done.4 = f32[256,2560]{1,0:T(8,128)} collective-permute-done((f32[256,2560]{1,0:T(8,128)S(1)}, f32[256,2560]{1,0:T(8,128)}, u32[]{:S(2)}, u32[]{:S(2)}) %collective-permute-start.4) | collective-permute-done | bytes 2621472 | tf_op jit(solution)/shard_map/ppermute | solution.py:49
  496.7 2.0 add.190
  498.8 0.7 multiply_reduce_fusion
  499.5 2.8 fusion.38
  502.5 2.4 fusion.37
  505.0 3.1 fusion.26
  508.4 3.3 convolution_add_fusion.3
  511.6 2.5 fusion.48
  514.4 2.6 convolution_add_fusion.2
  517.0 2.5 fusion.49
  519.8 2.6 convolution_add_fusion.1
  522.5 2.8 fusion.50
  525.5 3.7 fusion.1
  529.3 9.0 %slice.34 = bf16[32,64,2560]{2,1,0:T(8,128)(2,1)} slice(bf16[32,74,2560]{2,1,0:T(8,128)(2,1)} %all-gather.2.cloned.1.call-done), slice={[0:32], [0:64], [0:2560]} | slice | bytes 20971520 | tf_op jit(solution)/shard_map/slice | solution.py:102
  538.2 9.9 %gather_fusion = bf16[30,64,2560]{2,1,0:T(8,128)(2,1)} fusion(bf16[32,64,2560]{2,1,0:T(8,128)(2,1)} %slice.34, s32[1024]{0:T(1024)S(1)} %pad_clamp_fusion), kind=kCustom, calls=%fused_computation | custom fusion | bytes 19660920 | tf_op jit(solution)/shard_map/jit(_take)/gather | solution.py:102
  548.1 1.5 dynamic-slice_bitcast_fusion
  (60 shorter events, 11.6 us)
Async XLA Ops:
  7.2 522.1 %all-gather.2.cloned.1.call-start = ((), (), s32[]{:S(2)}) async-start(), calls=%async_computation.1 | async-start | bytes 13516800 | tf_op jit(solution)/shard_map/all_gather | solution.py:101
  14.2 1.1 copy-start.1
  190.2 6.9 %copy-start = (f32[1,74,2560]{2,0,1:T(1,128)S(1)}, f32[1,74,2560]{2,0,1:T(1,128)}, u32[]{:S(2)}) copy-start(f32[1,74,2560]{2,0,1:T(1,128)} %param.16) | copy-start | bytes 2273284
  209.4 3.1 copy-start.5
  210.1 18.5 %copy-start.2 = (bf16[128,2560]{1,0:T(8,128)(2,1)S(1)}, bf16[128,2560]{1,0:T(8,128)(2,1)}, u32[]{:S(2)}) copy-start(bf16[128,2560]{1,0:T(8,128)(2,1)} %param.9) | copy-start | bytes 1966084
  229.8 8.8 %collective-permute-start = (f32[256,2560]{1,0:T(8,128)S(1)}, f32[256,2560]{1,0:T(8,128)S(1)}, u32[]{:S(2)}, u32[]{:S(2)}) collective-permute-start(f32[256,2560]{1,0:T(8,128)S(1)} %fusion.47), channel_id=1, source_target_pairs={{0,4},{4,0},{8,12},{12,8},{16,20},{20,16},{24,28},{28,24},{32,36},... | collective-permute-start | bytes 7864328 | tf_op jit(solution)/shard_map/ppermute | solution.py:49
  238.9 84.5 %collective-permute-start.1 = (f32[256,2560]{1,0:T(8,128)S(1)}, f32[256,2560]{1,0:T(8,128)S(1)}, u32[]{:S(2)}, u32[]{:S(2)}) collective-permute-start(f32[256,2560]{1,0:T(8,128)S(1)} %add.186), channel_id=1, source_target_pairs={{0,8},{4,12},{8,0},{12,4},{16,24},{20,28},{24,16},{28,20},{32,40},... | collective-permute-start | bytes 7864328 | tf_op jit(solution)/shard_map/ppermute | solution.py:49
  323.7 58.8 %collective-permute-start.2 = (f32[256,2560]{1,0:T(8,128)S(1)}, f32[256,2560]{1,0:T(8,128)S(1)}, u32[]{:S(2)}, u32[]{:S(2)}) collective-permute-start(f32[256,2560]{1,0:T(8,128)S(1)} %add.187), channel_id=1, source_target_pairs={{0,16},{4,20},{8,24},{12,28},{16,0},{20,4},{24,8},{28,12},{32,48},... | collective-permute-start | bytes 7864328 | tf_op jit(solution)/shard_map/ppermute | solution.py:49
  382.8 56.4 %collective-permute-start.3 = (f32[256,2560]{1,0:T(8,128)S(1)}, f32[256,2560]{1,0:T(8,128)S(1)}, u32[]{:S(2)}, u32[]{:S(2)}) collective-permute-start(f32[256,2560]{1,0:T(8,128)S(1)} %add.188), channel_id=1, source_target_pairs={{0,32},{4,36},{8,40},{12,44},{16,48},{20,52},{24,56},{28,60},{32,0... | collective-permute-start | bytes 7864328 | tf_op jit(solution)/shard_map/ppermute | solution.py:49
  439.5 57.2 %collective-permute-start.4 = (f32[256,2560]{1,0:T(8,128)S(1)}, f32[256,2560]{1,0:T(8,128)}, u32[]{:S(2)}, u32[]{:S(2)}) collective-permute-start(f32[256,2560]{1,0:T(8,128)S(1)} %add.189), channel_id=1, source_target_pairs={{0,64},{4,68},{8,72},{12,76},{16,80},{20,84},{24,88},{28,92},{32,9... | collective-permute-start | bytes 7864328 | tf_op jit(solution)/shard_map/ppermute | solution.py:49
  445.3 53.4 %copy-start.3 = (f32[2,128,2560]{2,1,0:T(8,128)S(1)}, f32[2,128,2560]{2,1,0:T(8,128)}, u32[]{:S(2)}) copy-start(f32[2,128,2560]{2,1,0:T(8,128)} %param.17) | copy-start | bytes 7864324
  499.5 8.9 %copy-start.4 = (f32[2,128,2560]{2,1,0:T(8,128)}, f32[2,128,2560]{2,1,0:T(8,128)S(1)}, u32[]{:S(2)}) copy-start(f32[2,128,2560]{2,1,0:T(8,128)S(1)} %get-tuple-element.21) | copy-start | bytes 7864324
Sparse Core Ops, SparseCore 0:
  212.6 87.8 all-gather.1
